TPU v7x, 512 devices: a whole 4x4x16 slice. The times are simulated.
512 devices in a mesh: band: 8 (over x_lo, y), xy: 64 (over z, x_hi, core).
Axes of the slice: x: 4 (x_hi: 2, x_lo: 2; x = x_hi * 2 + x_lo), y: 4, z: 16, core: 2. Of those that a mesh axis runs over, the one named last changes fastest.
Arguments:
- orbitals: float32 [16, 64, 128, 256], P('band', 'xy'), may hold values from -6 to 6
- energies: float32 [16], P('band'), may hold values from -1.5 to -0.25
- occupation: int32 [16], P('band'), may hold values from 1 to 2
- potential: float32 [64, 128, 256], P('xy'), may hold values from 0.25 to 2
- trials: float32 [4, 64, 128, 256], P(None, 'xy'), may hold values from -8 to 23
Outputs:
- density: float32 [4, 64, 128, 256], P(None, 'xy', 'band')
- response_matrix: float32 [4, 4], replicated
All inputs are finite; a program needn't handle non-finite values.
Results may differ from a plain program's by a relative error of at most 0.0001.
Values sent between devices are 32-bit elements; how exact they have to be, the bound alone decides.
No kernel may reach another device: no remote copies, remote signals or barrier semaphores. Data moves between devices by JAX's collectives and lax.ppermute only.
A program may use at most 64 MiB of HBM per device.

v0:
```python
import math
import jax
import jax.numpy as jnp
from jax import lax
from jax.sharding import PartitionSpec as P

ITERS = 3


def padded_2(block, sides, width):
    for axis, dim in sides:
        count = lax.axis_size(axis)
        forward = [(i, i + 1) for i in range(count - 1)]
        forward.append((count - 1, 0))
        backward = [(target, source) for source, target in forward]
        low = lax.ppermute(
            lax.slice_in_dim(block, block.shape[dim] - width, None, axis=dim), axis, forward
        )
        high = lax.ppermute(lax.slice_in_dim(block, 0, width, axis=dim), axis, backward)
        block = jnp.concatenate([low, block, high], axis=dim)
    return block


def tree_sum(value, axes):
    for axis in axes:
        count = lax.axis_size(axis)
        step = 1
        while step < count:
            pairs = [(i, i ^ step) for i in range(count)]
            value = value + lax.ppermute(value, axis, pairs)
            step *= 2
    return value


def respond(psi_rows, energy_rows, weight_rows, potential_part, trial_part, project, apply_op):
    orbital_count, cell_count = psi_rows.shape
    trial_count = trial_part.shape[0]
    row_count = orbital_count * trial_count
    diagonal_op = 3.0 + potential_part.reshape(1, 1, cell_count) - energy_rows[:, None, None]
    diagonal_op = jnp.broadcast_to(diagonal_op, (orbital_count, trial_count, cell_count)).reshape(
        row_count, cell_count
    )
    products = trial_part[None, :, :] * psi_rows[:, None, :]
    right_side = -project(products.reshape(row_count, cell_count))
    update = project(right_side / diagonal_op)
    for iteration in range(ITERS):
        residual = right_side - apply_op(update, diagonal_op)
        update = update + project(residual / diagonal_op)
    weights = weight_rows[:, None, None] * psi_rows[:, None, :]
    return jnp.sum(weights * update.reshape(orbital_count, trial_count, cell_count), axis=0)


def neighbours_z(field_block):
    z_padded = jnp.pad(field_block, ((0, 0), (0, 0), (0, 0), (1, 1)))
    return z_padded[..., 2:] + z_padded[..., :-2]


def local(orbitals, energies, occupation, potential, trials):
    nb_dev, width_x, width_y, width_z = orbitals.shape
    trial_count = trials.shape[0]
    cell_count = width_x * width_y * width_z
    cell_total = cell_count * lax.axis_size("xy")
    orbital_total = nb_dev * lax.axis_size("band")
    y_share = width_y // lax.axis_size("band")
    band_index = lax.axis_index("band")
    highest = lax.Precision.HIGHEST
    trial_slice = lax.dynamic_slice_in_dim(trials, band_index * y_share, y_share, 2)
    psi_flat = orbitals.reshape(nb_dev, cell_count)
    psi_all = lax.all_gather(psi_flat, "band", axis=0, tiled=True)

    def project_slab(vectors):
        intersection = jnp.dot(
            psi_all, vectors.T, precision=highest, preferred_element_type=jnp.float32
        )
        intersection = tree_sum(intersection, ("xy",)) / cell_total
        return vectors - jnp.dot(
            intersection.T, psi_all, precision=highest, preferred_element_type=jnp.float32
        )

    def apply_slab(vectors, diagonal_op):
        field_block = vectors.reshape(-1, width_x, width_y, width_z)
        padded = padded_2(field_block, (("xy", 1),), 1)
        beside = padded[:, 2:] + padded[:, :-2]
        beside = beside + jnp.roll(field_block, 1, 2) + jnp.roll(field_block, -1, 2)
        beside = beside + neighbours_z(field_block)
        return diagonal_op * vectors - 0.5 * beside.reshape(vectors.shape)

    summed = respond(
        psi_flat,
        energies,
        occupation.astype(jnp.float32),
        potential.reshape(cell_count),
        trials.reshape(trial_count, cell_count),
        project_slab,
        apply_slab,
    )
    partial_grid = (summed / math.sqrt(orbital_total)).reshape(
        trial_count, width_x, width_y, width_z
    )
    density = lax.psum_scatter(partial_grid, "band", scatter_dimension=2, tiled=True)
    local_sum = jnp.dot(
        density.reshape(trial_count, -1),
        trial_slice.reshape(trial_count, -1).T,
        precision=highest,
        preferred_element_type=jnp.float32,
    )
    response_matrix = tree_sum(local_sum, ("band", "xy")) / cell_total
    return (density, response_matrix)


def solution(mesh):
    in_specs = (
        P("band", "xy", None, None),
        P("band"),
        P("band"),
        P("xy", None, None),
        P(None, "xy", None, None),
    )
    out_specs = (P(None, "xy", "band", None), P())
    return jax.shard_map(local, mesh=mesh, in_specs=in_specs, out_specs=out_specs, check_vma=False)
```

profile of v0, /device:TPU:4, one launch (start us, length us, event | category | flops | bytes accessed | tf_op | source)
XLA Modules:
  0.0 520.0 jit_solution(7207219664055754807)
XLA Ops:
  12.3 50.8 %all-gather.3.cloned.1.call-done = f32[8,2,32768]{2,1,0:T(2,128)} async-done(((f32[1,2,32768]{2,1,0:T(2,128)}), f32[8,2,32768]{2,1,0:T(2,128)}) %all-gather.3.cloned.1.call-update) | async-done | bytes 2097168 | tf_op jit(solution)/shard_map/all_gather | solution.py:69
  74.2 4.2 collective-permute-done.1
  78.4 3.5 collective-permute-start.2
  83.9 4.4 collective-permute-start.3
  90.3 7.6 %collective-permute-start.4 = (f32[16,8]{0,1:T(8,128)S(1)}, f32[16,8]{0,1:T(8,128)S(1)}, u32[]{:S(2)}, u32[]{:S(2)}) collective-permute-start(f32[16,8]{0,1:T(8,128)S(1)} %add.199), channel_id=1, source_target_pairs={{0,16},{1,17},{2,18},{3,19},{4,20},{5,21},{6,22},{7,23},{8,24},{9,... | collective-permute-start | bytes 1544 | tf_op jit(solution)/shard_map/ppermute | solution.py:30
  99.7 12.8 %collective-permute-start.5 = (f32[16,8]{0,1:T(8,128)S(1)}, f32[16,8]{0,1:T(8,128)S(1)}, u32[]{:S(2)}, u32[]{:S(2)}) collective-permute-start(f32[16,8]{0,1:T(8,128)S(1)} %add.200), channel_id=1, source_target_pairs={{0,32},{1,33},{2,34},{3,35},{4,36},{5,37},{6,38},{7,39},{8,40},{9,... | collective-permute-start | bytes 1544 | tf_op jit(solution)/shard_map/ppermute | solution.py:30
  126.3 4.2 collective-permute-done.7
  139.0 3.5 collective-permute-done.9
  142.5 6.0 %collective-permute-start.10 = (f32[16,8]{0,1:T(8,128)S(1)}, f32[16,8]{0,1:T(8,128)S(1)}, u32[]{:S(2)}, u32[]{:S(2)}) collective-permute-start(f32[16,8]{0,1:T(8,128)S(1)} %add.208), channel_id=1, source_target_pairs={{0,16},{1,17},{2,18},{3,19},{4,20},{5,21},{6,22},{7,23},{8,24},{9,... | collective-permute-start | bytes 1544 | tf_op jit(solution)/shard_map/ppermute | solution.py:30
  151.9 11.2 %collective-permute-start.11 = (f32[16,8]{0,1:T(8,128)S(1)}, f32[16,8]{0,1:T(8,128)S(1)}, u32[]{:S(2)}, u32[]{:S(2)}) collective-permute-start(f32[16,8]{0,1:T(8,128)S(1)} %add.209), channel_id=1, source_target_pairs={{0,32},{1,33},{2,34},{3,35},{4,36},{5,37},{6,38},{7,39},{8,40},{9,... | collective-permute-start | bytes 1544 | tf_op jit(solution)/shard_map/ppermute | solution.py:30
  171.9 20.8 %collective-permute-done.12 = f32[8,1,128,256]{3,0,2,1:T(8,128)S(1)} collective-permute-done((f32[8,1,128,256]{3,0,2,1:T(8,128)S(1)}, f32[8,1,128,256]{3,0,2,1:T(8,128)S(1)}, u32[]{:S(2)}, u32[]{:S(2)}) %collective-permute-start.12) | collective-permute-done | bytes 1048608 | tf_op jit(solution)/shard_map/ppermute | solution.py:19
  200.5 4.0 collective-permute-start.15
  213.0 4.5 collective-permute-start.17
  219.4 7.3 %collective-permute-start.18 = (f32[16,8]{0,1:T(8,128)S(1)}, f32[16,8]{0,1:T(8,128)S(1)}, u32[]{:S(2)}, u32[]{:S(2)}) collective-permute-start(f32[16,8]{0,1:T(8,128)S(1)} %add.219), channel_id=1, source_target_pairs={{0,16},{1,17},{2,18},{3,19},{4,20},{5,21},{6,22},{7,23},{8,24},{9,... | collective-permute-start | bytes 1544 | tf_op jit(solution)/shard_map/ppermute | solution.py:30
  228.8 11.2 %collective-permute-start.19 = (f32[16,8]{0,1:T(8,128)S(1)}, f32[16,8]{0,1:T(8,128)S(1)}, u32[]{:S(2)}, u32[]{:S(2)}) collective-permute-start(f32[16,8]{0,1:T(8,128)S(1)} %add.220), channel_id=1, source_target_pairs={{0,32},{1,33},{2,34},{3,35},{4,36},{5,37},{6,38},{7,39},{8,40},{9,... | collective-permute-start | bytes 1544 | tf_op jit(solution)/shard_map/ppermute | solution.py:30
  248.8 21.0 %collective-permute-done.20 = f32[8,1,128,256]{3,0,2,1:T(8,128)S(1)} collective-permute-done((f32[8,1,128,256]{3,0,2,1:T(8,128)S(1)}, f32[8,1,128,256]{3,0,2,1:T(8,128)S(1)}, u32[]{:S(2)}, u32[]{:S(2)}) %collective-permute-start.20) | collective-permute-done | bytes 1048608 | tf_op jit(solution)/shard_map/ppermute | solution.py:19
  281.5 4.2 collective-permute-done.23
  291.2 4.5 collective-permute-start.25
  297.6 7.3 %collective-permute-start.26 = (f32[16,8]{0,1:T(8,128)S(1)}, f32[16,8]{0,1:T(8,128)S(1)}, u32[]{:S(2)}, u32[]{:S(2)}) collective-permute-start(f32[16,8]{0,1:T(8,128)S(1)} %add.231), channel_id=1, source_target_pairs={{0,16},{1,17},{2,18},{3,19},{4,20},{5,21},{6,22},{7,23},{8,24},{9,... | collective-permute-start | bytes 1544 | tf_op jit(solution)/shard_map/ppermute | solution.py:30
  307.0 11.2 %collective-permute-start.27 = (f32[16,8]{0,1:T(8,128)S(1)}, f32[16,8]{0,1:T(8,128)S(1)}, u32[]{:S(2)}, u32[]{:S(2)}) collective-permute-start(f32[16,8]{0,1:T(8,128)S(1)} %add.232), channel_id=1, source_target_pairs={{0,32},{1,33},{2,34},{3,35},{4,36},{5,37},{6,38},{7,39},{8,40},{9,... | collective-permute-start | bytes 1544 | tf_op jit(solution)/shard_map/ppermute | solution.py:30
  327.0 21.0 %collective-permute-done.28 = f32[8,1,128,256]{3,0,2,1:T(8,128)S(1)} collective-permute-done((f32[8,1,128,256]{3,0,2,1:T(8,128)S(1)}, f32[8,1,128,256]{3,0,2,1:T(8,128)S(1)}, u32[]{:S(2)}, u32[]{:S(2)}) %collective-permute-start.28) | collective-permute-done | bytes 1048608 | tf_op jit(solution)/shard_map/ppermute | solution.py:19
  359.7 4.1 collective-permute-done.31
  369.3 4.8 collective-permute-start.33
  375.7 7.6 %collective-permute-start.34 = (f32[16,8]{0,1:T(8,128)S(1)}, f32[16,8]{0,1:T(8,128)S(1)}, u32[]{:S(2)}, u32[]{:S(2)}) collective-permute-start(f32[16,8]{0,1:T(8,128)S(1)} %add.243), channel_id=1, source_target_pairs={{0,16},{1,17},{2,18},{3,19},{4,20},{5,21},{6,22},{7,23},{8,24},{9,... | collective-permute-start | bytes 1544 | tf_op jit(solution)/shard_map/ppermute | solution.py:30
  385.1 10.2 %collective-permute-start.35 = (f32[16,8]{0,1:T(8,128)S(1)}, f32[16,8]{0,1:T(8,128)S(1)}, u32[]{:S(2)}, u32[]{:S(2)}) collective-permute-start(f32[16,8]{0,1:T(8,128)S(1)} %add.244), channel_id=1, source_target_pairs={{0,32},{1,33},{2,34},{3,35},{4,36},{5,37},{6,38},{7,39},{8,40},{9,... | collective-permute-start | bytes 1544 | tf_op jit(solution)/shard_map/ppermute | solution.py:30
  405.5 42.3 %reduce-scatter.2.cloned.1.call-done = f32[4,1,16,256]{3,2,1,0:T(8,128)} async-done(((f32[4,1,128,256]{3,2,1,0:T(8,128)}), f32[4,1,16,256]{3,2,1,0:T(8,128)}) %reduce-scatter.2.cloned.1.call-update) | async-done | bytes 65552 | tf_op jit(solution)/shard_map/reduce_scatter | solution.py:100
  451.0 3.6 collective-permute-done.36
  457.3 4.2 collective-permute-done.37
  472.8 4.2 collective-permute-done.40
  482.5 4.4 collective-permute-start.42
  488.8 7.6 %collective-permute-start.43 = (f32[4,4]{1,0:T(4,128)S(1)}, f32[4,4]{1,0:T(4,128)S(1)}, u32[]{:S(2)}, u32[]{:S(2)}) collective-permute-start(f32[4,4]{1,0:T(4,128)S(1)} %add.254), channel_id=1, source_target_pairs={{0,16},{1,17},{2,18},{3,19},{4,20},{5,21},{6,22},{7,23},{8,24},{9,... | collective-permute-start | bytes 200 | tf_op jit(solution)/shard_map/ppermute | solution.py:30
  498.2 12.8 %collective-permute-start.44 = (f32[4,4]{1,0:T(4,128)S(1)}, f32[4,4]{1,0:T(4,128)S(1)}, u32[]{:S(2)}, u32[]{:S(2)}) collective-permute-start(f32[4,4]{1,0:T(4,128)S(1)} %add.255), channel_id=1, source_target_pairs={{0,32},{1,33},{2,34},{3,35},{4,36},{5,37},{6,38},{7,39},{8,40},{9,... | collective-permute-start | bytes 200 | tf_op jit(solution)/shard_map/ppermute | solution.py:30
  (146 shorter events, 174.1 us)
Async XLA Ops:
  7.2 55.9 %all-gather.3.cloned.1.call-start = ((), (), s32[]{:S(2)}) async-start(), calls=%async_computation.2 | async-start | bytes 2359296 | tf_op jit(solution)/shard_map/all_gather | solution.py:69
  9.0 438.7 %reduce-scatter.2.cloned.1.call-start = ((), (), s32[]{:S(2)}) async-start(), calls=%async_computation.1 | async-start | bytes 589824 | tf_op jit(solution)/shard_map/reduce_scatter | solution.py:100
  71.4 7.0 %collective-permute-start.1 = (f32[16,8]{0,1:T(8,128)S(1)}, f32[16,8]{0,1:T(8,128)S(1)}, u32[]{:S(2)}, u32[]{:S(2)}) collective-permute-start(f32[16,8]{0,1:T(8,128)S(1)} %add.196), channel_id=1, source_target_pairs={{0,2},{1,3},{2,0},{3,1},{4,6},{5,7},{6,4},{7,5},{8,10},{9,11},{10,... | collective-permute-start | bytes 1544 | tf_op jit(solution)/shard_map/ppermute | solution.py:30
  83.9 6.4 %collective-permute-start.3 = (f32[16,8]{0,1:T(8,128)S(1)}, f32[16,8]{0,1:T(8,128)S(1)}, u32[]{:S(2)}, u32[]{:S(2)}) collective-permute-start(f32[16,8]{0,1:T(8,128)S(1)} %add.198), channel_id=1, source_target_pairs={{0,8},{1,9},{2,10},{3,11},{4,12},{5,13},{6,14},{7,15},{8,0},{9,1},... | collective-permute-start | bytes 1544 | tf_op jit(solution)/shard_map/ppermute | solution.py:30
  90.3 9.4 %collective-permute-start.4 = (f32[16,8]{0,1:T(8,128)S(1)}, f32[16,8]{0,1:T(8,128)S(1)}, u32[]{:S(2)}, u32[]{:S(2)}) collective-permute-start(f32[16,8]{0,1:T(8,128)S(1)} %add.199), channel_id=1, source_target_pairs={{0,16},{1,17},{2,18},{3,19},{4,20},{5,21},{6,22},{7,23},{8,24},{9,... | collective-permute-start | bytes 1544 | tf_op jit(solution)/shard_map/ppermute | solution.py:30
  99.7 15.8 %collective-permute-start.5 = (f32[16,8]{0,1:T(8,128)S(1)}, f32[16,8]{0,1:T(8,128)S(1)}, u32[]{:S(2)}, u32[]{:S(2)}) collective-permute-start(f32[16,8]{0,1:T(8,128)S(1)} %add.200), channel_id=1, source_target_pairs={{0,32},{1,33},{2,34},{3,35},{4,36},{5,37},{6,38},{7,39},{8,40},{9,... | collective-permute-start | bytes 1544 | tf_op jit(solution)/shard_map/ppermute | solution.py:30
  123.6 7.0 %collective-permute-start.7 = (f32[16,8]{0,1:T(8,128)S(1)}, f32[16,8]{0,1:T(8,128)S(1)}, u32[]{:S(2)}, u32[]{:S(2)}) collective-permute-start(f32[16,8]{0,1:T(8,128)S(1)} %add.205), channel_id=1, source_target_pairs={{0,2},{1,3},{2,0},{3,1},{4,6},{5,7},{6,4},{7,5},{8,10},{9,11},{10,... | collective-permute-start | bytes 1544 | tf_op jit(solution)/shard_map/ppermute | solution.py:30
  136.1 6.4 %collective-permute-start.9 = (f32[16,8]{0,1:T(8,128)S(1)}, f32[16,8]{0,1:T(8,128)S(1)}, u32[]{:S(2)}, u32[]{:S(2)}) collective-permute-start(f32[16,8]{0,1:T(8,128)S(1)} %add.207), channel_id=1, source_target_pairs={{0,8},{1,9},{2,10},{3,11},{4,12},{5,13},{6,14},{7,15},{8,0},{9,1},... | collective-permute-start | bytes 1544 | tf_op jit(solution)/shard_map/ppermute | solution.py:30
  142.5 9.4 %collective-permute-start.10 = (f32[16,8]{0,1:T(8,128)S(1)}, f32[16,8]{0,1:T(8,128)S(1)}, u32[]{:S(2)}, u32[]{:S(2)}) collective-permute-start(f32[16,8]{0,1:T(8,128)S(1)} %add.208), channel_id=1, source_target_pairs={{0,16},{1,17},{2,18},{3,19},{4,20},{5,21},{6,22},{7,23},{8,24},{9,... | collective-permute-start | bytes 1544 | tf_op jit(solution)/shard_map/ppermute | solution.py:30
  151.9 14.2 %collective-permute-start.11 = (f32[16,8]{0,1:T(8,128)S(1)}, f32[16,8]{0,1:T(8,128)S(1)}, u32[]{:S(2)}, u32[]{:S(2)}) collective-permute-start(f32[16,8]{0,1:T(8,128)S(1)} %add.209), channel_id=1, source_target_pairs={{0,32},{1,33},{2,34},{3,35},{4,36},{5,37},{6,38},{7,39},{8,40},{9,... | collective-permute-start | bytes 1544 | tf_op jit(solution)/shard_map/ppermute | solution.py:30
  167.2 25.5 %collective-permute-start.12 = (f32[8,1,128,256]{3,0,2,1:T(8,128)S(1)}, f32[8,1,128,256]{3,0,2,1:T(8,128)S(1)}, u32[]{:S(2)}, u32[]{:S(2)}) collective-permute-start(f32[8,1,128,256]{3,0,2,1:T(8,128)S(1)} %bitcast.55), channel_id=1, source_target_pairs={{1,0},{2,1},{3,2},{4,3},{5,4},{6,5},{7,6},{8,7},{9,8},{10,9},{11,1... | collective-permute-start | bytes 3145736 | tf_op jit(solution)/shard_map/ppermute | solution.py:19
  169.2 24.9 %collective-permute-start.13 = (f32[8,1,128,256]{3,0,2,1:T(8,128)S(1)}, f32[8,1,128,256]{3,0,2,1:T(8,128)S(1)}, u32[]{:S(2)}, u32[]{:S(2)}) collective-permute-start(f32[8,1,128,256]{3,0,2,1:T(8,128)S(1)} %bitcast.56), channel_id=1, source_target_pairs={{0,1},{1,2},{2,3},{3,4},{4,5},{5,6},{6,7},{7,8},{8,9},{9,10},{10,1... | collective-permute-start | bytes 3145736 | tf_op jit(solution)/shard_map/ppermute | solution.py:16
  200.5 7.0 %collective-permute-start.15 = (f32[16,8]{0,1:T(8,128)S(1)}, f32[16,8]{0,1:T(8,128)S(1)}, u32[]{:S(2)}, u32[]{:S(2)}) collective-permute-start(f32[16,8]{0,1:T(8,128)S(1)} %add.216), channel_id=1, source_target_pairs={{0,2},{1,3},{2,0},{3,1},{4,6},{5,7},{6,4},{7,5},{8,10},{9,11},{10,... | collective-permute-start | bytes 1544 | tf_op jit(solution)/shard_map/ppermute | solution.py:30
  213.0 6.4 %collective-permute-start.17 = (f32[16,8]{0,1:T(8,128)S(1)}, f32[16,8]{0,1:T(8,128)S(1)}, u32[]{:S(2)}, u32[]{:S(2)}) collective-permute-start(f32[16,8]{0,1:T(8,128)S(1)} %add.218), channel_id=1, source_target_pairs={{0,8},{1,9},{2,10},{3,11},{4,12},{5,13},{6,14},{7,15},{8,0},{9,1},... | collective-permute-start | bytes 1544 | tf_op jit(solution)/shard_map/ppermute | solution.py:30
  219.4 9.4 %collective-permute-start.18 = (f32[16,8]{0,1:T(8,128)S(1)}, f32[16,8]{0,1:T(8,128)S(1)}, u32[]{:S(2)}, u32[]{:S(2)}) collective-permute-start(f32[16,8]{0,1:T(8,128)S(1)} %add.219), channel_id=1, source_target_pairs={{0,16},{1,17},{2,18},{3,19},{4,20},{5,21},{6,22},{7,23},{8,24},{9,... | collective-permute-start | bytes 1544 | tf_op jit(solution)/shard_map/ppermute | solution.py:30
  228.8 14.2 %collective-permute-start.19 = (f32[16,8]{0,1:T(8,128)S(1)}, f32[16,8]{0,1:T(8,128)S(1)}, u32[]{:S(2)}, u32[]{:S(2)}) collective-permute-start(f32[16,8]{0,1:T(8,128)S(1)} %add.220), channel_id=1, source_target_pairs={{0,32},{1,33},{2,34},{3,35},{4,36},{5,37},{6,38},{7,39},{8,40},{9,... | collective-permute-start | bytes 1544 | tf_op jit(solution)/shard_map/ppermute | solution.py:30
  244.3 25.5 %collective-permute-start.20 = (f32[8,1,128,256]{3,0,2,1:T(8,128)S(1)}, f32[8,1,128,256]{3,0,2,1:T(8,128)S(1)}, u32[]{:S(2)}, u32[]{:S(2)}) collective-permute-start(f32[8,1,128,256]{3,0,2,1:T(8,128)S(1)} %bitcast.60), channel_id=1, source_target_pairs={{1,0},{2,1},{3,2},{4,3},{5,4},{6,5},{7,6},{8,7},{9,8},{10,9},{11,1... | collective-permute-start | bytes 3145736 | tf_op jit(solution)/shard_map/ppermute | solution.py:19
  246.2 26.1 %collective-permute-start.21 = (f32[8,1,128,256]{3,0,2,1:T(8,128)S(1)}, f32[8,1,128,256]{3,0,2,1:T(8,128)S(1)}, u32[]{:S(2)}, u32[]{:S(2)}) collective-permute-start(f32[8,1,128,256]{3,0,2,1:T(8,128)S(1)} %bitcast.61), channel_id=1, source_target_pairs={{0,1},{1,2},{2,3},{3,4},{4,5},{5,6},{6,7},{7,8},{8,9},{9,10},{10,1... | collective-permute-start | bytes 3145736 | tf_op jit(solution)/shard_map/ppermute | solution.py:16
  278.7 7.0 %collective-permute-start.23 = (f32[16,8]{0,1:T(8,128)S(1)}, f32[16,8]{0,1:T(8,128)S(1)}, u32[]{:S(2)}, u32[]{:S(2)}) collective-permute-start(f32[16,8]{0,1:T(8,128)S(1)} %add.228), channel_id=1, source_target_pairs={{0,2},{1,3},{2,0},{3,1},{4,6},{5,7},{6,4},{7,5},{8,10},{9,11},{10,... | collective-permute-start | bytes 1544 | tf_op jit(solution)/shard_map/ppermute | solution.py:30
  291.2 6.4 %collective-permute-start.25 = (f32[16,8]{0,1:T(8,128)S(1)}, f32[16,8]{0,1:T(8,128)S(1)}, u32[]{:S(2)}, u32[]{:S(2)}) collective-permute-start(f32[16,8]{0,1:T(8,128)S(1)} %add.230), channel_id=1, source_target_pairs={{0,8},{1,9},{2,10},{3,11},{4,12},{5,13},{6,14},{7,15},{8,0},{9,1},... | collective-permute-start | bytes 1544 | tf_op jit(solution)/shard_map/ppermute | solution.py:30
  297.6 9.4 %collective-permute-start.26 = (f32[16,8]{0,1:T(8,128)S(1)}, f32[16,8]{0,1:T(8,128)S(1)}, u32[]{:S(2)}, u32[]{:S(2)}) collective-permute-start(f32[16,8]{0,1:T(8,128)S(1)} %add.231), channel_id=1, source_target_pairs={{0,16},{1,17},{2,18},{3,19},{4,20},{5,21},{6,22},{7,23},{8,24},{9,... | collective-permute-start | bytes 1544 | tf_op jit(solution)/shard_map/ppermute | solution.py:30
  307.0 14.2 %collective-permute-start.27 = (f32[16,8]{0,1:T(8,128)S(1)}, f32[16,8]{0,1:T(8,128)S(1)}, u32[]{:S(2)}, u32[]{:S(2)}) collective-permute-start(f32[16,8]{0,1:T(8,128)S(1)} %add.232), channel_id=1, source_target_pairs={{0,32},{1,33},{2,34},{3,35},{4,36},{5,37},{6,38},{7,39},{8,40},{9,... | collective-permute-start | bytes 1544 | tf_op jit(solution)/shard_map/ppermute | solution.py:30
  322.5 25.5 %collective-permute-start.28 = (f32[8,1,128,256]{3,0,2,1:T(8,128)S(1)}, f32[8,1,128,256]{3,0,2,1:T(8,128)S(1)}, u32[]{:S(2)}, u32[]{:S(2)}) collective-permute-start(f32[8,1,128,256]{3,0,2,1:T(8,128)S(1)} %bitcast.50), channel_id=1, source_target_pairs={{1,0},{2,1},{3,2},{4,3},{5,4},{6,5},{7,6},{8,7},{9,8},{10,9},{11,1... | collective-permute-start | bytes 3145736 | tf_op jit(solution)/shard_map/ppermute | solution.py:19
  324.4 26.0 %collective-permute-start.29 = (f32[8,1,128,256]{3,0,2,1:T(8,128)S(1)}, f32[8,1,128,256]{3,0,2,1:T(8,128)S(1)}, u32[]{:S(2)}, u32[]{:S(2)}) collective-permute-start(f32[8,1,128,256]{3,0,2,1:T(8,128)S(1)} %bitcast.51), channel_id=1, source_target_pairs={{0,1},{1,2},{2,3},{3,4},{4,5},{5,6},{6,7},{7,8},{8,9},{9,10},{10,1... | collective-permute-start | bytes 3145736 | tf_op jit(solution)/shard_map/ppermute | solution.py:16
  356.8 7.0 %collective-permute-start.31 = (f32[16,8]{0,1:T(8,128)S(1)}, f32[16,8]{0,1:T(8,128)S(1)}, u32[]{:S(2)}, u32[]{:S(2)}) collective-permute-start(f32[16,8]{0,1:T(8,128)S(1)} %add.240), channel_id=1, source_target_pairs={{0,2},{1,3},{2,0},{3,1},{4,6},{5,7},{6,4},{7,5},{8,10},{9,11},{10,... | collective-permute-start | bytes 1544 | tf_op jit(solution)/shard_map/ppermute | solution.py:30
  369.3 6.4 %collective-permute-start.33 = (f32[16,8]{0,1:T(8,128)S(1)}, f32[16,8]{0,1:T(8,128)S(1)}, u32[]{:S(2)}, u32[]{:S(2)}) collective-permute-start(f32[16,8]{0,1:T(8,128)S(1)} %add.242), channel_id=1, source_target_pairs={{0,8},{1,9},{2,10},{3,11},{4,12},{5,13},{6,14},{7,15},{8,0},{9,1},... | collective-permute-start | bytes 1544 | tf_op jit(solution)/shard_map/ppermute | solution.py:30
  375.7 9.4 %collective-permute-start.34 = (f32[16,8]{0,1:T(8,128)S(1)}, f32[16,8]{0,1:T(8,128)S(1)}, u32[]{:S(2)}, u32[]{:S(2)}) collective-permute-start(f32[16,8]{0,1:T(8,128)S(1)} %add.243), channel_id=1, source_target_pairs={{0,16},{1,17},{2,18},{3,19},{4,20},{5,21},{6,22},{7,23},{8,24},{9,... | collective-permute-start | bytes 1544 | tf_op jit(solution)/shard_map/ppermute | solution.py:30
  385.1 14.2 %collective-permute-start.35 = (f32[16,8]{0,1:T(8,128)S(1)}, f32[16,8]{0,1:T(8,128)S(1)}, u32[]{:S(2)}, u32[]{:S(2)}) collective-permute-start(f32[16,8]{0,1:T(8,128)S(1)} %add.244), channel_id=1, source_target_pairs={{0,32},{1,33},{2,34},{3,35},{4,36},{5,37},{6,38},{7,39},{8,40},{9,... | collective-permute-start | bytes 1544 | tf_op jit(solution)/shard_map/ppermute | solution.py:30
  454.5 7.0 %collective-permute-start.37 = (f32[4,4]{1,0:T(4,128)S(1)}, f32[4,4]{1,0:T(4,128)S(1)}, u32[]{:S(2)}, u32[]{:S(2)}) collective-permute-start(f32[4,4]{1,0:T(4,128)S(1)} %add.248), channel_id=1, source_target_pairs={{0,128},{64,192},{128,0},{192,64},{256,384},{320,448},{384,256},{4... | collective-permute-start | bytes 200 | tf_op jit(solution)/shard_map/ppermute | solution.py:30
  470.0 7.0 %collective-permute-start.40 = (f32[4,4]{1,0:T(4,128)S(1)}, f32[4,4]{1,0:T(4,128)S(1)}, u32[]{:S(2)}, u32[]{:S(2)}) collective-permute-start(f32[4,4]{1,0:T(4,128)S(1)} %add.251), channel_id=1, source_target_pairs={{0,2},{1,3},{2,0},{3,1},{4,6},{5,7},{6,4},{7,5},{8,10},{9,11},{10,... | collective-permute-start | bytes 200 | tf_op jit(solution)/shard_map/ppermute | solution.py:30
  488.8 9.4 %collective-permute-start.43 = (f32[4,4]{1,0:T(4,128)S(1)}, f32[4,4]{1,0:T(4,128)S(1)}, u32[]{:S(2)}, u32[]{:S(2)}) collective-permute-start(f32[4,4]{1,0:T(4,128)S(1)} %add.254), channel_id=1, source_target_pairs={{0,16},{1,17},{2,18},{3,19},{4,20},{5,21},{6,22},{7,23},{8,24},{9,... | collective-permute-start | bytes 200 | tf_op jit(solution)/shard_map/ppermute | solution.py:30
  498.2 14.4 %collective-permute-start.44 = (f32[4,4]{1,0:T(4,128)S(1)}, f32[4,4]{1,0:T(4,128)S(1)}, u32[]{:S(2)}, u32[]{:S(2)}) collective-permute-start(f32[4,4]{1,0:T(4,128)S(1)} %add.255), channel_id=1, source_target_pairs={{0,32},{1,33},{2,34},{3,35},{4,36},{5,37},{6,38},{7,39},{8,40},{9,... | collective-permute-start | bytes 200 | tf_op jit(solution)/shard_map/ppermute | solution.py:30
  (20 other events, 281.9 us)
Sparse Core Ops, SparseCore 0:
  10.0 53.0 all-gather.2
  404.7 42.9 reduce-scatter.1
where the time goes:
time: 522 us; the launch traced here: 520 us
  waiting for transfers between devices  257 us (49%)
  starting transfers between devices  207 us (40%)
  matrix products  22.8 us (4%)
  between operations  14.7 us (3%)
  local copies, waits for them, and re-layouts  14 us (3%)
    ppermute x39, starting transfers between devices, tree_sum(): value = value + lax.ppermute(value, axis, pairs)  194 us
    ppermute x39, waiting for transfers between devices, tree_sum(): value = value + lax.ppermute(value, axis, pairs)  94.4 us
    ppermute x3, waiting for transfers between devices, padded_2(): lax.ppermute(lax.slice_in_dim(block, 0, width, axis=dim), axis, backward)  62.7 us
    all_gather x1, waiting for transfers between devices, local(): psi_all = lax.all_gather(psi_flat, 'band', axis=0, tiled=True)  50.8 us
    reduce_scatter x1, waiting for transfers between devices, local(): lax.psum_scatter(partial_grid, 'band', scatter_dimension=2, tiled=True)  42.3 us
    dot_general x5, matrix products, project_slab(): jnp.dot(psi_all, vectors.T, precision=highest, preferred_element_type=jnp...  13.1 us
  transfers between devices with their start and end apart: 47, of which 46 were waited for; matrix products, arithmetic and copies ran while one was open for 2% of the time, Pallas kernels for 0%

commit v1 on v0

--- a/solution.py
+++ b/solution.py
@@ -3,6 +3,7 @@
 import jax.numpy as jnp
 from jax import lax
 from jax.sharding import PartitionSpec as P
+from jax.lax import all_to_all, psum
 
 ITERS = 3
 
@@ -66,7 +67,15 @@
     highest = lax.Precision.HIGHEST
     trial_slice = lax.dynamic_slice_in_dim(trials, band_index * y_share, y_share, 2)
     psi_flat = orbitals.reshape(nb_dev, cell_count)
-    psi_all = lax.all_gather(psi_flat, "band", axis=0, tiled=True)
+    psi_all = jnp.concatenate(
+        all_to_all(
+            jnp.stack(psum(1, axis_name="band") * [psi_flat], axis=0),
+            axis_name="band",
+            split_axis=0,
+            concat_axis=0,
+        ),
+        axis=0,
+    )
 
     def project_slab(vectors):
         intersection = jnp.dot(

time: 522 us -> 504 us (0.966)
  waiting for transfers between devices: 257 us -> 233 us
  starting transfers between devices: 207 us -> 214 us
    all_gather x1 -> x0, waiting for transfers between devices: 50.8 us -> none  [local(): psi_all = lax.all_gather(psi_flat, 'band', axis=0, tiled=True)]
    all_to_all x0 -> x1, waiting for transfers between devices: none -> 25.1 us  [local(): all_to_all(jnp.stack(psum(1, axis_name='band') * [psi_flat], axis=0), axi...]
    unnamed x16, local copies, waits for them, and re-layouts: 8.04 us -> 2.49 us
    all_to_all x0 -> x1, starting transfers between devices: none -> 5.24 us  [local(): all_to_all(jnp.stack(psum(1, axis_name='band') * [psi_flat], axis=0), axi...]
  transfers between devices with their start and end apart: 47 -> 47, of which waited for: 46 -> 46; matrix products, arithmetic and copies ran while one was open for 2% -> 1% of each run, Pallas kernels for 0% -> 0%
where the time goes in v1:
time: 504 us; the launch traced here: 502 us
  waiting for transfers between devices  233 us (46%)
  starting transfers between devices  214 us (42%)
  matrix products  22.8 us (5%)
  between operations  14.7 us (3%)
  local copies, waits for them, and re-layouts  13.1 us (3%)
    ppermute x39, starting transfers between devices, tree_sum(): value = value + lax.ppermute(value, axis, pairs)  196 us
    ppermute x39, waiting for transfers between devices, tree_sum(): value = value + lax.ppermute(value, axis, pairs)  95.6 us
    ppermute x3, waiting for transfers between devices, padded_2(): lax.ppermute(lax.slice_in_dim(block, 0, width, axis=dim), axis, backward)  62.7 us
    reduce_scatter x1, waiting for transfers between devices, local(): lax.psum_scatter(partial_grid, 'band', scatter_dimension=2, tiled=True)  43.3 us
    all_to_all x1, waiting for transfers between devices, local(): all_to_all(jnp.stack(psum(1, axis_name='band') * [psi_flat], axis=0), axi...  25.1 us
    dot_general x5, matrix products, project_slab(): jnp.dot(psi_all, vectors.T, precision=highest, preferred_element_type=jnp...  13.1 us
  transfers between devices with their start and end apart: 47, of which 46 were waited for; matrix products, arithmetic and copies ran while one was open for 1% of the time, Pallas kernels for 0%

profile of v1, /device:TPU:4, one launch (start us, length us, event | category | flops | bytes accessed | tf_op | source)
XLA Modules:
  0.0 502.5 jit_solution(18177670900014711793)
XLA Ops:
  10.2 5.2 %all-to-all-start = ((f32[8,2,32768]{2,1,0:T(2,128)}), f32[8,2,32768]{2,1,0:T(2,128)}, u32[]{:S(2)}, u32[]{:S(2)}) async-start(f32[8,2,32768]{2,1,0:T(2,128)} %stack.3), calls=%async_computation | async-start | bytes 4194304 | tf_op jit(solution)/shard_map/all_to_all | solution.py:71
  16.5 25.1 %all-to-all-done = f32[8,2,32768]{2,1,0:T(2,128)} async-done(((f32[8,2,32768]{2,1,0:T(2,128)}), f32[8,2,32768]{2,1,0:T(2,128)}, u32[]{:S(2)}, u32[]{:S(2)}) %all-to-all-start) | async-done | bytes 2097184 | tf_op jit(solution)/shard_map/all_to_all | solution.py:71
  52.7 4.3 collective-permute-done.1
  57.0 3.8 collective-permute-start.2
  62.4 5.2 %collective-permute-start.3 = (f32[16,8]{0,1:T(8,128)S(1)}, f32[16,8]{0,1:T(8,128)S(1)}, u32[]{:S(2)}, u32[]{:S(2)}) collective-permute-start(f32[16,8]{0,1:T(8,128)S(1)} %add.198), channel_id=1, source_target_pairs={{0,8},{1,9},{2,10},{3,11},{4,12},{5,13},{6,14},{7,15},{8,0},{9,1},... | collective-permute-start | bytes 1544 | tf_op jit(solution)/shard_map/ppermute | solution.py:31
  69.2 9.1 %collective-permute-start.4 = (f32[16,8]{0,1:T(8,128)S(1)}, f32[16,8]{0,1:T(8,128)S(1)}, u32[]{:S(2)}, u32[]{:S(2)}) collective-permute-start(f32[16,8]{0,1:T(8,128)S(1)} %add.199), channel_id=1, source_target_pairs={{0,16},{1,17},{2,18},{3,19},{4,20},{5,21},{6,22},{7,23},{8,24},{9,... | collective-permute-start | bytes 1544 | tf_op jit(solution)/shard_map/ppermute | solution.py:31
  79.9 14.1 %collective-permute-start.5 = (f32[16,8]{0,1:T(8,128)S(1)}, f32[16,8]{0,1:T(8,128)S(1)}, u32[]{:S(2)}, u32[]{:S(2)}) collective-permute-start(f32[16,8]{0,1:T(8,128)S(1)} %add.200), channel_id=1, source_target_pairs={{0,32},{1,33},{2,34},{3,35},{4,36},{5,37},{6,38},{7,39},{8,40},{9,... | collective-permute-start | bytes 1544 | tf_op jit(solution)/shard_map/ppermute | solution.py:31
  107.7 4.3 collective-permute-done.7
  123.9 5.0 collective-permute-start.10
  128.9 4.4 collective-permute-done.10
  133.3 11.2 %collective-permute-start.11 = (f32[16,8]{0,1:T(8,128)S(1)}, f32[16,8]{0,1:T(8,128)S(1)}, u32[]{:S(2)}, u32[]{:S(2)}) collective-permute-start(f32[16,8]{0,1:T(8,128)S(1)} %add.209), channel_id=1, source_target_pairs={{0,32},{1,33},{2,34},{3,35},{4,36},{5,37},{6,38},{7,39},{8,40},{9,... | collective-permute-start | bytes 1544 | tf_op jit(solution)/shard_map/ppermute | solution.py:31
  153.3 20.8 %collective-permute-done.12 = f32[8,1,128,256]{3,0,2,1:T(8,128)S(1)} collective-permute-done((f32[8,1,128,256]{3,0,2,1:T(8,128)S(1)}, f32[8,1,128,256]{3,0,2,1:T(8,128)S(1)}, u32[]{:S(2)}, u32[]{:S(2)}) %collective-permute-start.12) | collective-permute-done | bytes 1048608 | tf_op jit(solution)/shard_map/ppermute | solution.py:20
  182.2 3.7 collective-permute-start.15
  201.1 7.0 %collective-permute-start.18 = (f32[16,8]{0,1:T(8,128)S(1)}, f32[16,8]{0,1:T(8,128)S(1)}, u32[]{:S(2)}, u32[]{:S(2)}) collective-permute-start(f32[16,8]{0,1:T(8,128)S(1)} %add.219), channel_id=1, source_target_pairs={{0,16},{1,17},{2,18},{3,19},{4,20},{5,21},{6,22},{7,23},{8,24},{9,... | collective-permute-start | bytes 1544 | tf_op jit(solution)/shard_map/ppermute | solution.py:31
  210.5 11.2 %collective-permute-start.19 = (f32[16,8]{0,1:T(8,128)S(1)}, f32[16,8]{0,1:T(8,128)S(1)}, u32[]{:S(2)}, u32[]{:S(2)}) collective-permute-start(f32[16,8]{0,1:T(8,128)S(1)} %add.220), channel_id=1, source_target_pairs={{0,32},{1,33},{2,34},{3,35},{4,36},{5,37},{6,38},{7,39},{8,40},{9,... | collective-permute-start | bytes 1544 | tf_op jit(solution)/shard_map/ppermute | solution.py:31
  230.5 21.0 %collective-permute-done.20 = f32[8,1,128,256]{3,0,2,1:T(8,128)S(1)} collective-permute-done((f32[8,1,128,256]{3,0,2,1:T(8,128)S(1)}, f32[8,1,128,256]{3,0,2,1:T(8,128)S(1)}, u32[]{:S(2)}, u32[]{:S(2)}) %collective-permute-start.20) | collective-permute-done | bytes 1048608 | tf_op jit(solution)/shard_map/ppermute | solution.py:20
  263.2 4.3 collective-permute-done.23
  279.4 7.0 %collective-permute-start.26 = (f32[16,8]{0,1:T(8,128)S(1)}, f32[16,8]{0,1:T(8,128)S(1)}, u32[]{:S(2)}, u32[]{:S(2)}) collective-permute-start(f32[16,8]{0,1:T(8,128)S(1)} %add.231), channel_id=1, source_target_pairs={{0,16},{1,17},{2,18},{3,19},{4,20},{5,21},{6,22},{7,23},{8,24},{9,... | collective-permute-start | bytes 1544 | tf_op jit(solution)/shard_map/ppermute | solution.py:31
  288.8 11.2 %collective-permute-start.27 = (f32[16,8]{0,1:T(8,128)S(1)}, f32[16,8]{0,1:T(8,128)S(1)}, u32[]{:S(2)}, u32[]{:S(2)}) collective-permute-start(f32[16,8]{0,1:T(8,128)S(1)} %add.232), channel_id=1, source_target_pairs={{0,32},{1,33},{2,34},{3,35},{4,36},{5,37},{6,38},{7,39},{8,40},{9,... | collective-permute-start | bytes 1544 | tf_op jit(solution)/shard_map/ppermute | solution.py:31
  308.8 21.0 %collective-permute-done.28 = f32[8,1,128,256]{3,0,2,1:T(8,128)S(1)} collective-permute-done((f32[8,1,128,256]{3,0,2,1:T(8,128)S(1)}, f32[8,1,128,256]{3,0,2,1:T(8,128)S(1)}, u32[]{:S(2)}, u32[]{:S(2)}) %collective-permute-start.28) | collective-permute-done | bytes 1048608 | tf_op jit(solution)/shard_map/ppermute | solution.py:20
  338.0 3.5 collective-permute-start.31
  341.5 3.5 collective-permute-done.31
  350.5 5.0 collective-permute-start.33
  357.1 7.6 %collective-permute-start.34 = (f32[16,8]{0,1:T(8,128)S(1)}, f32[16,8]{0,1:T(8,128)S(1)}, u32[]{:S(2)}, u32[]{:S(2)}) collective-permute-start(f32[16,8]{0,1:T(8,128)S(1)} %add.243), channel_id=1, source_target_pairs={{0,16},{1,17},{2,18},{3,19},{4,20},{5,21},{6,22},{7,23},{8,24},{9,... | collective-permute-start | bytes 1544 | tf_op jit(solution)/shard_map/ppermute | solution.py:31
  366.5 10.9 %collective-permute-start.35 = (f32[16,8]{0,1:T(8,128)S(1)}, f32[16,8]{0,1:T(8,128)S(1)}, u32[]{:S(2)}, u32[]{:S(2)}) collective-permute-start(f32[16,8]{0,1:T(8,128)S(1)} %add.244), channel_id=1, source_target_pairs={{0,32},{1,33},{2,34},{3,35},{4,36},{5,37},{6,38},{7,39},{8,40},{9,... | collective-permute-start | bytes 1544 | tf_op jit(solution)/shard_map/ppermute | solution.py:31
  386.9 43.3 %reduce-scatter.2.cloned.1.call-done = f32[4,1,16,256]{3,2,1,0:T(8,128)} async-done(((f32[4,1,128,256]{3,2,1,0:T(8,128)}), f32[4,1,16,256]{3,2,1,0:T(8,128)}) %reduce-scatter.2.cloned.1.call-update) | async-done | bytes 65552 | tf_op jit(solution)/shard_map/reduce_scatter | solution.py:109
  433.4 3.6 collective-permute-done.36
  439.7 4.2 collective-permute-done.37
  455.2 4.3 collective-permute-done.40
  464.9 4.4 collective-permute-start.42
  471.3 7.6 %collective-permute-start.43 = (f32[4,4]{1,0:T(4,128)S(1)}, f32[4,4]{1,0:T(4,128)S(1)}, u32[]{:S(2)}, u32[]{:S(2)}) collective-permute-start(f32[4,4]{1,0:T(4,128)S(1)} %add.254), channel_id=1, source_target_pairs={{0,16},{1,17},{2,18},{3,19},{4,20},{5,21},{6,22},{7,23},{8,24},{9,... | collective-permute-start | bytes 200 | tf_op jit(solution)/shard_map/ppermute | solution.py:31
  480.7 12.8 %collective-permute-start.44 = (f32[4,4]{1,0:T(4,128)S(1)}, f32[4,4]{1,0:T(4,128)S(1)}, u32[]{:S(2)}, u32[]{:S(2)}) collective-permute-start(f32[4,4]{1,0:T(4,128)S(1)} %add.255), channel_id=1, source_target_pairs={{0,32},{1,33},{2,34},{3,35},{4,36},{5,37},{6,38},{7,39},{8,40},{9,... | collective-permute-start | bytes 200 | tf_op jit(solution)/shard_map/ppermute | solution.py:31
  (147 shorter events, 178.3 us)
Async XLA Ops:
  10.2 31.4 %all-to-all-start = ((f32[8,2,32768]{2,1,0:T(2,128)}), f32[8,2,32768]{2,1,0:T(2,128)}, u32[]{:S(2)}, u32[]{:S(2)}) async-start(f32[8,2,32768]{2,1,0:T(2,128)} %stack.3), calls=%async_computation | async-start | bytes 4194304 | tf_op jit(solution)/shard_map/all_to_all | solution.py:71
  15.5 414.7 %reduce-scatter.2.cloned.1.call-start = ((), (), s32[]{:S(2)}) async-start(), calls=%async_computation.2 | async-start | bytes 589824 | tf_op jit(solution)/shard_map/reduce_scatter | solution.py:109
  50.0 7.0 %collective-permute-start.1 = (f32[16,8]{0,1:T(8,128)S(1)}, f32[16,8]{0,1:T(8,128)S(1)}, u32[]{:S(2)}, u32[]{:S(2)}) collective-permute-start(f32[16,8]{0,1:T(8,128)S(1)} %add.196), channel_id=1, source_target_pairs={{0,2},{1,3},{2,0},{3,1},{4,6},{5,7},{6,4},{7,5},{8,10},{9,11},{10,... | collective-permute-start | bytes 1544 | tf_op jit(solution)/shard_map/ppermute | solution.py:31
  62.4 6.7 %collective-permute-start.3 = (f32[16,8]{0,1:T(8,128)S(1)}, f32[16,8]{0,1:T(8,128)S(1)}, u32[]{:S(2)}, u32[]{:S(2)}) collective-permute-start(f32[16,8]{0,1:T(8,128)S(1)} %add.198), channel_id=1, source_target_pairs={{0,8},{1,9},{2,10},{3,11},{4,12},{5,13},{6,14},{7,15},{8,0},{9,1},... | collective-permute-start | bytes 1544 | tf_op jit(solution)/shard_map/ppermute | solution.py:31
  69.2 10.7 %collective-permute-start.4 = (f32[16,8]{0,1:T(8,128)S(1)}, f32[16,8]{0,1:T(8,128)S(1)}, u32[]{:S(2)}, u32[]{:S(2)}) collective-permute-start(f32[16,8]{0,1:T(8,128)S(1)} %add.199), channel_id=1, source_target_pairs={{0,16},{1,17},{2,18},{3,19},{4,20},{5,21},{6,22},{7,23},{8,24},{9,... | collective-permute-start | bytes 1544 | tf_op jit(solution)/shard_map/ppermute | solution.py:31
  79.9 17.0 %collective-permute-start.5 = (f32[16,8]{0,1:T(8,128)S(1)}, f32[16,8]{0,1:T(8,128)S(1)}, u32[]{:S(2)}, u32[]{:S(2)}) collective-permute-start(f32[16,8]{0,1:T(8,128)S(1)} %add.200), channel_id=1, source_target_pairs={{0,32},{1,33},{2,34},{3,35},{4,36},{5,37},{6,38},{7,39},{8,40},{9,... | collective-permute-start | bytes 1544 | tf_op jit(solution)/shard_map/ppermute | solution.py:31
  105.0 7.0 %collective-permute-start.7 = (f32[16,8]{0,1:T(8,128)S(1)}, f32[16,8]{0,1:T(8,128)S(1)}, u32[]{:S(2)}, u32[]{:S(2)}) collective-permute-start(f32[16,8]{0,1:T(8,128)S(1)} %add.205), channel_id=1, source_target_pairs={{0,2},{1,3},{2,0},{3,1},{4,6},{5,7},{6,4},{7,5},{8,10},{9,11},{10,... | collective-permute-start | bytes 1544 | tf_op jit(solution)/shard_map/ppermute | solution.py:31
  117.5 6.4 %collective-permute-start.9 = (f32[16,8]{0,1:T(8,128)S(1)}, f32[16,8]{0,1:T(8,128)S(1)}, u32[]{:S(2)}, u32[]{:S(2)}) collective-permute-start(f32[16,8]{0,1:T(8,128)S(1)} %add.207), channel_id=1, source_target_pairs={{0,8},{1,9},{2,10},{3,11},{4,12},{5,13},{6,14},{7,15},{8,0},{9,1},... | collective-permute-start | bytes 1544 | tf_op jit(solution)/shard_map/ppermute | solution.py:31
  123.9 9.4 %collective-permute-start.10 = (f32[16,8]{0,1:T(8,128)S(1)}, f32[16,8]{0,1:T(8,128)S(1)}, u32[]{:S(2)}, u32[]{:S(2)}) collective-permute-start(f32[16,8]{0,1:T(8,128)S(1)} %add.208), channel_id=1, source_target_pairs={{0,16},{1,17},{2,18},{3,19},{4,20},{5,21},{6,22},{7,23},{8,24},{9,... | collective-permute-start | bytes 1544 | tf_op jit(solution)/shard_map/ppermute | solution.py:31
  133.3 14.2 %collective-permute-start.11 = (f32[16,8]{0,1:T(8,128)S(1)}, f32[16,8]{0,1:T(8,128)S(1)}, u32[]{:S(2)}, u32[]{:S(2)}) collective-permute-start(f32[16,8]{0,1:T(8,128)S(1)} %add.209), channel_id=1, source_target_pairs={{0,32},{1,33},{2,34},{3,35},{4,36},{5,37},{6,38},{7,39},{8,40},{9,... | collective-permute-start | bytes 1544 | tf_op jit(solution)/shard_map/ppermute | solution.py:31
  148.6 25.5 %collective-permute-start.12 = (f32[8,1,128,256]{3,0,2,1:T(8,128)S(1)}, f32[8,1,128,256]{3,0,2,1:T(8,128)S(1)}, u32[]{:S(2)}, u32[]{:S(2)}) collective-permute-start(f32[8,1,128,256]{3,0,2,1:T(8,128)S(1)} %bitcast.53), channel_id=1, source_target_pairs={{1,0},{2,1},{3,2},{4,3},{5,4},{6,5},{7,6},{8,7},{9,8},{10,9},{11,1... | collective-permute-start | bytes 3145736 | tf_op jit(solution)/shard_map/ppermute | solution.py:20
  150.6 25.2 %collective-permute-start.13 = (f32[8,1,128,256]{3,0,2,1:T(8,128)S(1)}, f32[8,1,128,256]{3,0,2,1:T(8,128)S(1)}, u32[]{:S(2)}, u32[]{:S(2)}) collective-permute-start(f32[8,1,128,256]{3,0,2,1:T(8,128)S(1)} %bitcast.54), channel_id=1, source_target_pairs={{0,1},{1,2},{2,3},{3,4},{4,5},{5,6},{6,7},{7,8},{8,9},{9,10},{10,1... | collective-permute-start | bytes 3145736 | tf_op jit(solution)/shard_map/ppermute | solution.py:17
  182.2 7.0 %collective-permute-start.15 = (f32[16,8]{0,1:T(8,128)S(1)}, f32[16,8]{0,1:T(8,128)S(1)}, u32[]{:S(2)}, u32[]{:S(2)}) collective-permute-start(f32[16,8]{0,1:T(8,128)S(1)} %add.216), channel_id=1, source_target_pairs={{0,2},{1,3},{2,0},{3,1},{4,6},{5,7},{6,4},{7,5},{8,10},{9,11},{10,... | collective-permute-start | bytes 1544 | tf_op jit(solution)/shard_map/ppermute | solution.py:31
  194.7 6.4 %collective-permute-start.17 = (f32[16,8]{0,1:T(8,128)S(1)}, f32[16,8]{0,1:T(8,128)S(1)}, u32[]{:S(2)}, u32[]{:S(2)}) collective-permute-start(f32[16,8]{0,1:T(8,128)S(1)} %add.218), channel_id=1, source_target_pairs={{0,8},{1,9},{2,10},{3,11},{4,12},{5,13},{6,14},{7,15},{8,0},{9,1},... | collective-permute-start | bytes 1544 | tf_op jit(solution)/shard_map/ppermute | solution.py:31
  201.1 9.4 %collective-permute-start.18 = (f32[16,8]{0,1:T(8,128)S(1)}, f32[16,8]{0,1:T(8,128)S(1)}, u32[]{:S(2)}, u32[]{:S(2)}) collective-permute-start(f32[16,8]{0,1:T(8,128)S(1)} %add.219), channel_id=1, source_target_pairs={{0,16},{1,17},{2,18},{3,19},{4,20},{5,21},{6,22},{7,23},{8,24},{9,... | collective-permute-start | bytes 1544 | tf_op jit(solution)/shard_map/ppermute | solution.py:31
  210.5 14.2 %collective-permute-start.19 = (f32[16,8]{0,1:T(8,128)S(1)}, f32[16,8]{0,1:T(8,128)S(1)}, u32[]{:S(2)}, u32[]{:S(2)}) collective-permute-start(f32[16,8]{0,1:T(8,128)S(1)} %add.220), channel_id=1, source_target_pairs={{0,32},{1,33},{2,34},{3,35},{4,36},{5,37},{6,38},{7,39},{8,40},{9,... | collective-permute-start | bytes 1544 | tf_op jit(solution)/shard_map/ppermute | solution.py:31
  226.0 25.5 %collective-permute-start.20 = (f32[8,1,128,256]{3,0,2,1:T(8,128)S(1)}, f32[8,1,128,256]{3,0,2,1:T(8,128)S(1)}, u32[]{:S(2)}, u32[]{:S(2)}) collective-permute-start(f32[8,1,128,256]{3,0,2,1:T(8,128)S(1)} %bitcast.58), channel_id=1, source_target_pairs={{1,0},{2,1},{3,2},{4,3},{5,4},{6,5},{7,6},{8,7},{9,8},{10,9},{11,1... | collective-permute-start | bytes 3145736 | tf_op jit(solution)/shard_map/ppermute | solution.py:20
  227.9 26.2 %collective-permute-start.21 = (f32[8,1,128,256]{3,0,2,1:T(8,128)S(1)}, f32[8,1,128,256]{3,0,2,1:T(8,128)S(1)}, u32[]{:S(2)}, u32[]{:S(2)}) collective-permute-start(f32[8,1,128,256]{3,0,2,1:T(8,128)S(1)} %bitcast.59), channel_id=1, source_target_pairs={{0,1},{1,2},{2,3},{3,4},{4,5},{5,6},{6,7},{7,8},{8,9},{9,10},{10,1... | collective-permute-start | bytes 3145736 | tf_op jit(solution)/shard_map/ppermute | solution.py:17
  260.5 7.0 %collective-permute-start.23 = (f32[16,8]{0,1:T(8,128)S(1)}, f32[16,8]{0,1:T(8,128)S(1)}, u32[]{:S(2)}, u32[]{:S(2)}) collective-permute-start(f32[16,8]{0,1:T(8,128)S(1)} %add.228), channel_id=1, source_target_pairs={{0,2},{1,3},{2,0},{3,1},{4,6},{5,7},{6,4},{7,5},{8,10},{9,11},{10,... | collective-permute-start | bytes 1544 | tf_op jit(solution)/shard_map/ppermute | solution.py:31
  273.0 6.4 %collective-permute-start.25 = (f32[16,8]{0,1:T(8,128)S(1)}, f32[16,8]{0,1:T(8,128)S(1)}, u32[]{:S(2)}, u32[]{:S(2)}) collective-permute-start(f32[16,8]{0,1:T(8,128)S(1)} %add.230), channel_id=1, source_target_pairs={{0,8},{1,9},{2,10},{3,11},{4,12},{5,13},{6,14},{7,15},{8,0},{9,1},... | collective-permute-start | bytes 1544 | tf_op jit(solution)/shard_map/ppermute | solution.py:31
  279.4 9.4 %collective-permute-start.26 = (f32[16,8]{0,1:T(8,128)S(1)}, f32[16,8]{0,1:T(8,128)S(1)}, u32[]{:S(2)}, u32[]{:S(2)}) collective-permute-start(f32[16,8]{0,1:T(8,128)S(1)} %add.231), channel_id=1, source_target_pairs={{0,16},{1,17},{2,18},{3,19},{4,20},{5,21},{6,22},{7,23},{8,24},{9,... | collective-permute-start | bytes 1544 | tf_op jit(solution)/shard_map/ppermute | solution.py:31
  288.8 14.2 %collective-permute-start.27 = (f32[16,8]{0,1:T(8,128)S(1)}, f32[16,8]{0,1:T(8,128)S(1)}, u32[]{:S(2)}, u32[]{:S(2)}) collective-permute-start(f32[16,8]{0,1:T(8,128)S(1)} %add.232), channel_id=1, source_target_pairs={{0,32},{1,33},{2,34},{3,35},{4,36},{5,37},{6,38},{7,39},{8,40},{9,... | collective-permute-start | bytes 1544 | tf_op jit(solution)/shard_map/ppermute | solution.py:31
  304.3 25.5 %collective-permute-start.28 = (f32[8,1,128,256]{3,0,2,1:T(8,128)S(1)}, f32[8,1,128,256]{3,0,2,1:T(8,128)S(1)}, u32[]{:S(2)}, u32[]{:S(2)}) collective-permute-start(f32[8,1,128,256]{3,0,2,1:T(8,128)S(1)} %bitcast.48), channel_id=1, source_target_pairs={{1,0},{2,1},{3,2},{4,3},{5,4},{6,5},{7,6},{8,7},{9,8},{10,9},{11,1... | collective-permute-start | bytes 3145736 | tf_op jit(solution)/shard_map/ppermute | solution.py:20
  306.2 25.4 %collective-permute-start.29 = (f32[8,1,128,256]{3,0,2,1:T(8,128)S(1)}, f32[8,1,128,256]{3,0,2,1:T(8,128)S(1)}, u32[]{:S(2)}, u32[]{:S(2)}) collective-permute-start(f32[8,1,128,256]{3,0,2,1:T(8,128)S(1)} %bitcast.49), channel_id=1, source_target_pairs={{0,1},{1,2},{2,3},{3,4},{4,5},{5,6},{6,7},{7,8},{8,9},{9,10},{10,1... | collective-permute-start | bytes 3145736 | tf_op jit(solution)/shard_map/ppermute | solution.py:17
  338.0 7.0 %collective-permute-start.31 = (f32[16,8]{0,1:T(8,128)S(1)}, f32[16,8]{0,1:T(8,128)S(1)}, u32[]{:S(2)}, u32[]{:S(2)}) collective-permute-start(f32[16,8]{0,1:T(8,128)S(1)} %add.240), channel_id=1, source_target_pairs={{0,2},{1,3},{2,0},{3,1},{4,6},{5,7},{6,4},{7,5},{8,10},{9,11},{10,... | collective-permute-start | bytes 1544 | tf_op jit(solution)/shard_map/ppermute | solution.py:31
  350.5 6.6 %collective-permute-start.33 = (f32[16,8]{0,1:T(8,128)S(1)}, f32[16,8]{0,1:T(8,128)S(1)}, u32[]{:S(2)}, u32[]{:S(2)}) collective-permute-start(f32[16,8]{0,1:T(8,128)S(1)} %add.242), channel_id=1, source_target_pairs={{0,8},{1,9},{2,10},{3,11},{4,12},{5,13},{6,14},{7,15},{8,0},{9,1},... | collective-permute-start | bytes 1544 | tf_op jit(solution)/shard_map/ppermute | solution.py:31
  357.1 9.4 %collective-permute-start.34 = (f32[16,8]{0,1:T(8,128)S(1)}, f32[16,8]{0,1:T(8,128)S(1)}, u32[]{:S(2)}, u32[]{:S(2)}) collective-permute-start(f32[16,8]{0,1:T(8,128)S(1)} %add.243), channel_id=1, source_target_pairs={{0,16},{1,17},{2,18},{3,19},{4,20},{5,21},{6,22},{7,23},{8,24},{9,... | collective-permute-start | bytes 1544 | tf_op jit(solution)/shard_map/ppermute | solution.py:31
  366.5 14.2 %collective-permute-start.35 = (f32[16,8]{0,1:T(8,128)S(1)}, f32[16,8]{0,1:T(8,128)S(1)}, u32[]{:S(2)}, u32[]{:S(2)}) collective-permute-start(f32[16,8]{0,1:T(8,128)S(1)} %add.244), channel_id=1, source_target_pairs={{0,32},{1,33},{2,34},{3,35},{4,36},{5,37},{6,38},{7,39},{8,40},{9,... | collective-permute-start | bytes 1544 | tf_op jit(solution)/shard_map/ppermute | solution.py:31
  437.0 7.0 %collective-permute-start.37 = (f32[4,4]{1,0:T(4,128)S(1)}, f32[4,4]{1,0:T(4,128)S(1)}, u32[]{:S(2)}, u32[]{:S(2)}) collective-permute-start(f32[4,4]{1,0:T(4,128)S(1)} %add.248), channel_id=1, source_target_pairs={{0,128},{64,192},{128,0},{192,64},{256,384},{320,448},{384,256},{4... | collective-permute-start | bytes 200 | tf_op jit(solution)/shard_map/ppermute | solution.py:31
  452.5 7.0 %collective-permute-start.40 = (f32[4,4]{1,0:T(4,128)S(1)}, f32[4,4]{1,0:T(4,128)S(1)}, u32[]{:S(2)}, u32[]{:S(2)}) collective-permute-start(f32[4,4]{1,0:T(4,128)S(1)} %add.251), channel_id=1, source_target_pairs={{0,2},{1,3},{2,0},{3,1},{4,6},{5,7},{6,4},{7,5},{8,10},{9,11},{10,... | collective-permute-start | bytes 200 | tf_op jit(solution)/shard_map/ppermute | solution.py:31
  471.3 9.4 %collective-permute-start.43 = (f32[4,4]{1,0:T(4,128)S(1)}, f32[4,4]{1,0:T(4,128)S(1)}, u32[]{:S(2)}, u32[]{:S(2)}) collective-permute-start(f32[4,4]{1,0:T(4,128)S(1)} %add.254), channel_id=1, source_target_pairs={{0,16},{1,17},{2,18},{3,19},{4,20},{5,21},{6,22},{7,23},{8,24},{9,... | collective-permute-start | bytes 200 | tf_op jit(solution)/shard_map/ppermute | solution.py:31
  480.7 14.4 %collective-permute-start.44 = (f32[4,4]{1,0:T(4,128)S(1)}, f32[4,4]{1,0:T(4,128)S(1)}, u32[]{:S(2)}, u32[]{:S(2)}) collective-permute-start(f32[4,4]{1,0:T(4,128)S(1)} %add.255), channel_id=1, source_target_pairs={{0,32},{1,33},{2,34},{3,35},{4,36},{5,37},{6,38},{7,39},{8,40},{9,... | collective-permute-start | bytes 200 | tf_op jit(solution)/shard_map/ppermute | solution.py:31
  (21 other events, 219.4 us)
Sparse Core Ops, SparseCore 0:
  386.1 44.0 reduce-scatter.1
